TPU v7x, 32 devices: a whole 2x2x4 slice. The times are simulated.
32 devices in a mesh: groups: 2 (over y), tm: 4 (over z), space: 2 (over x), dp: 2 (over core).
Axes of the slice: x: 2, y: 2, z: 4, core: 2. Of those that a mesh axis runs over, the one named last changes fastest.
Arguments:
- video_input: bfloat16 [4, 4, 8, 256, 96], P(('groups', 'dp'), 'tm', 'space'), parts along dimension 0, may hold values from -48 to 48
- out_cotangent: bfloat16 [4, 4, 8, 256, 96], P(('groups', 'dp'), 'tm', 'space'), parts along dimension 0, may hold values from -6 to 6
- conv_weight: bfloat16 [3, 3, 3, 96, 96], replicated, may hold values from -0.125 to 0.125
- sketch_signs: int32 [2, 96, 32], replicated, may hold values from 0 to 1
Outputs:
- input_grad: bfloat16 [4, 4, 8, 256, 96], P(('groups', 'dp'), 'tm', 'space'), parts along dimension 0
- weight_grad: float32 [6, 3, 3, 96, 96], P('groups'), parts along dimension 0
- sketches: float32 [4, 96, 32], P('groups'), parts along dimension 0
There are 2 independent parts, one for each index of `groups`. A program takes and returns all parts, laid end to end along the dimension named above; an argument that names none is the same for every part. Nothing has to cross between parts.
All inputs are finite; a program needn't handle non-finite values.
Results may differ from a plain program's by a relative error of at most 0.0025.
Values may be sent and summed in bfloat16 or wider, within the bound.
No kernel may reach another device: no remote copies, remote signals or barrier semaphores. Data moves between devices by JAX's collectives and lax.ppermute only.
A program may use at most 64 MiB of HBM per device.

v0:
```python
import jax
import jax.numpy as jnp
from jax import lax
from jax.sharding import PartitionSpec as P


def padded(value, sides, width):
    for axis, dim in sides:
        peers, length = (lax.axis_size(axis), value.shape[dim])
        up = [(i, (i + 1) % peers) for i in range(peers - 1)]
        down = [(j, i) for i, j in up]
        last = lax.slice_in_dim(value, length - width, length, axis=dim)
        leading = lax.slice_in_dim(value, 0, width, axis=dim)
        before = lax.ppermute(last, axis, up)
        after = lax.ppermute(leading, axis, down)
        value = jnp.concatenate([before, value, after], axis=dim)
    return value


def passed_along(block, axis, distance):
    devices = range(lax.axis_size(axis))
    route = [(i - distance, i) for i in devices if i - distance in devices]
    return lax.ppermute(block, axis, route)


def silu_slope(value):
    sig = jax.nn.sigmoid(value)
    return sig * (1.0 + value * (1.0 - sig))


def pad_columns(field):
    return jnp.pad(field, ((0, 0), (0, 0), (1, 1), (0, 0)))


def contract_rows(left, right):
    return lax.dot_general(
        left, right, (((0,), (0,)), ((), ())), preferred_element_type=jnp.float32
    )


def on_device(video_input, out_cotangent, conv_weight, sketch_signs):
    xin = video_input[:, 0]
    grad_out = out_cotangent[:, 0]
    batch, rows, width, chans = xin.shape
    count = batch * rows * width
    hidden = jax.nn.silu(xin.astype(jnp.float32)).astype(jnp.bfloat16)
    hid_flat = hidden.reshape(count, chans)
    grad_flat = grad_out.reshape(count, chans)
    grad_rows = padded(grad_out, (("space", 1),), 1)
    grad_frames = [pad_columns(grad_rows)]
    for lag in (1, 2):
        grad_frames.append(pad_columns(passed_along(grad_rows, "tm", -lag)))
    hid_rows = padded(hidden, (("space", 1),), 1)
    hid_frames = [pad_columns(hid_rows)]
    for lag in (1, 2):
        hid_frames.append(pad_columns(passed_along(hid_rows, "tm", lag)))
    grad_hidden = jnp.zeros((count, chans), jnp.float32)
    kernel_terms = []
    for a in range(3):
        for b in range(3):
            source = grad_frames[2 - a]
            slab = jnp.concatenate(
                [source[:, 2 - b : 2 - b + rows, 2 - e : 2 - e + width, :] for e in range(3)],
                axis=-1,
            ).reshape(count, 3 * chans)
            weight_mat = jnp.transpose(conv_weight[a, b], (0, 2, 1)).reshape(3 * chans, chans)
            grad_hidden = grad_hidden + jnp.dot(
                slab, weight_mat, preferred_element_type=jnp.float32
            )
            earlier = hid_frames[2 - a]
            hid_slab = jnp.concatenate(
                [earlier[:, b : b + rows, e : e + width, :] for e in range(3)], axis=-1
            ).reshape(count, 3 * chans)
            kernel_terms.append(contract_rows(hid_slab, grad_flat).reshape(3, chans, chans))
    kernel_local = jnp.stack(kernel_terms).reshape(3, 3, 3, chans, chans)
    xflat = xin.reshape(count, chans).astype(jnp.float32)
    input_grad = (grad_hidden * silu_slope(xflat)).astype(jnp.bfloat16)
    input_grad = input_grad.reshape(batch, 1, rows, width, chans)
    omega = (2 * sketch_signs - 1).astype(jnp.float32)
    cov_hidden = contract_rows(hid_flat, hid_flat)
    cov_grad = contract_rows(grad_flat, grad_flat)
    sketch_terms = jnp.stack(
        [
            jnp.dot(cov_hidden, omega[0], precision=lax.Precision.HIGHEST),
            jnp.dot(cov_grad, omega[1], precision=lax.Precision.HIGHEST),
        ]
    )
    total_pixels = (
        count
        * video_input.shape[1]
        * lax.axis_size("tm")
        * lax.axis_size("space")
        * lax.axis_size("dp")
    )
    sketch_total = lax.psum(sketch_terms, ("tm", "space", "dp"))
    kernel_total = lax.psum(kernel_local, ("tm", "space", "dp"))
    sketches = sketch_total / jnp.float32(total_pixels)
    weight_grad = kernel_total * (1.0 / jnp.sqrt(jnp.float32(total_pixels)))
    return (input_grad, weight_grad, sketches)


def solution(mesh):
    in_specs = (
        P(("groups", "dp"), "tm", "space", None, None),
        P(("groups", "dp"), "tm", "space", None, None),
        P(),
        P(),
    )
    out_specs = (
        P(("groups", "dp"), "tm", "space", None, None),
        P("groups", None, None, None, None),
        P("groups", None, None),
    )
    return jax.shard_map(
        on_device, mesh=mesh, in_specs=in_specs, out_specs=out_specs, check_vma=False
    )
```

profile of v0, /device:TPU:0, one launch (start us, length us, event | category | flops | bytes accessed | tf_op | source)
XLA Modules:
  0.0 231.1 jit_solution(7625184018858395198)
XLA Ops:
  7.2 0.9 fusion.34
  8.2 1.3 collective-permute-start.1
  9.4 4.9 %collective-permute-start = (bf16[1,1,256,96]{2,3,1,0:T(8,128)(2,1)S(1)}, bf16[1,1,256,96]{2,3,1,0:T(8,128)(2,1)S(1)}, u32[]{:S(2)}, u32[]{:S(2)}) collective-permute-start(bf16[1,1,256,96]{2,3,1,0:T(8,128)(2,1)S(1)} %get-tuple-element.72), channel_id=1, source_target_pairs={{0,2},{1,3},{4,6},{5,7},{8,10},{9,11},{12,14},{13,15},{16,18},{17,... | collective-permute-start | bytes 147464 | tf_op jit(solution)/shard_map/ppermute | solution.py:14
  14.3 1.0 fusion.27
  15.4 1.3 collective-permute-start.5
  16.7 4.5 %collective-permute-start.4 = (bf16[1,1,256,96]{2,3,1,0:T(8,128)(2,1)S(1)}, bf16[1,1,256,96]{2,3,1,0:T(8,128)(2,1)S(1)}, u32[]{:S(2)}, u32[]{:S(2)}) collective-permute-start(bf16[1,1,256,96]{2,3,1,0:T(8,128)(2,1)S(1)} %get-tuple-element.68), channel_id=1, source_target_pairs={{0,2},{1,3},{4,6},{5,7},{8,10},{9,11},{12,14},{13,15},{16,18},{17,... | collective-permute-start | bytes 147464 | tf_op jit(solution)/shard_map/ppermute | solution.py:14
  21.2 1.1 copy.31
  24.6 59.7 %psum.15 = f32[2,96,32]{1,2,0:T(8,128)S(1)} all-reduce(f32[2,96,32]{1,2,0:T(8,128)S(1)} %pad_maximum_fusion.19), channel_id=1, replica_groups=mesh['groups'=2,'tm'=4,'space'=2,'dp'=2] {'tm','space','dp'}, use_global_device_ids=true, to_apply=%region_1.2 | all-reduce | flops 6144 | bytes 49152 | tf_op jit(solution)/shard_map/psum | solution.py:95
  85.1 0.7 copy.43
  85.8 0.7 copy.44
  86.6 0.7 copy.45
  87.3 0.7 copy.46
  88.0 0.7 copy.47
  88.8 0.7 copy.48
  89.5 0.7 copy.49
  90.2 0.7 copy.50
  91.1 0.7 copy.60
  91.8 0.7 copy.51
  92.5 1.3 collective-permute-start.2
  93.8 1.3 collective-permute-start.3
  95.6 6.1 %collective-permute-start.6 = (bf16[1,6,256,96]{2,3,1,0:T(8,128)(2,1)S(1)}, bf16[1,6,256,96]{2,3,1,0:T(8,128)(2,1)S(1)}, u32[]{:S(2)}, u32[]{:S(2)}) collective-permute-start(bf16[1,6,256,96]{2,3,1,0:T(8,128)(2,1)S(1)} %pad_maximum_fusion.18), channel_id=1, source_target_pairs={{0,8},{4,12},{1,9},{5,13},{2,10},{6,14},{3,11},{7,15},{16,24},{20,... | collective-permute-start | bytes 884744 | tf_op jit(solution)/shard_map/ppermute | solution.py:23
  101.7 4.1 %collective-permute-start.7 = (bf16[1,6,256,96]{2,3,1,0:T(8,128)(2,1)S(1)}, bf16[1,6,256,96]{2,3,1,0:T(8,128)(2,1)S(1)}, u32[]{:S(2)}, u32[]{:S(2)}) collective-permute-start(bf16[1,6,256,96]{2,3,1,0:T(8,128)(2,1)S(1)} %pad_maximum_fusion.18), channel_id=1, source_target_pairs={{0,4},{4,8},{8,12},{1,5},{5,9},{9,13},{2,6},{6,10},{10,14},{3,7},{... | collective-permute-start | bytes 884744 | tf_op jit(solution)/shard_map/ppermute | solution.py:23
  107.7 0.7 copy.61
  108.5 0.7 copy.59
  109.7 0.9 copy.62
  116.2 0.9 copy.56
  117.6 0.9 copy.57
  125.8 1.1 copy-done.3
  126.9 1.2 fusion.35
  132.4 0.7 copy.42
  133.1 88.6 %all-reduce.8.cloned.1.call-done = f32[3,3,3,96,96]{4,3,2,1,0:T(8,128)} async-done(((f32[3,3,3,96,96]{4,3,2,1,0:T(8,128)}), f32[3,3,3,96,96]{4,3,2,1,0:T(8,128)}) %all-reduce.8.cloned.1.call-update) | async-done | bytes 995344 | tf_op jit(solution)/shard_map/psum | solution.py:96
  221.7 2.5 %broadcast_multiply_fusion = f32[3,3,3,96,96]{4,3,2,1,0:T(8,128)} fusion(f32[3,3,3,96,96]{4,3,2,1,0:T(8,128)} %all-reduce.8.cloned.1.call-done), kind=kLoop, calls=%fused_computation.32 | loop fusion | flops 248832 | bytes 1990656 | tf_op jit(solution)/shard_map/mul | solution.py:98
  (132 shorter events, 23.1 us)
Async XLA Ops:
  7.2 15.2 %copy-start = (bf16[1,1,4,256,96]{3,4,2,1,0:T(8,128)(2,1)S(1)}, bf16[1,1,4,256,96]{3,4,2,1,0:T(8,128)(2,1)}, u32[]{:S(2)}) copy-start(bf16[1,1,4,256,96]{3,4,2,1,0:T(8,128)(2,1)} %param.5) | copy-start | bytes 589828
  7.2 15.4 %copy-start.4 = (bf16[1,1,4,256,96]{3,4,2,1,0:T(8,128)(2,1)S(1)}, bf16[1,1,4,256,96]{3,4,2,1,0:T(8,128)(2,1)}, u32[]{:S(2)}) copy-start(bf16[1,1,4,256,96]{3,4,2,1,0:T(8,128)(2,1)} %param.4) | copy-start | bytes 589828
  7.2 214.5 %all-reduce.8.cloned.1.call-start = ((), (), s32[]{:S(2)}) async-start(), calls=%async_computation | async-start | bytes 2654208 | tf_op jit(solution)/shard_map/psum | solution.py:96
  8.2 84.3 %collective-permute-start.1 = (bf16[1,1,256,96]{2,3,1,0:T(8,128)(2,1)S(1)}, bf16[1,1,256,96]{2,3,1,0:T(8,128)(2,1)S(1)}, u32[]{:S(2)}, u32[]{:S(2)}) collective-permute-start(bf16[1,1,256,96]{2,3,1,0:T(8,128)(2,1)S(1)} %get-tuple-element.73), channel_id=1, source_target_pairs={{2,0},{3,1},{6,4},{7,5},{10,8},{11,9},{14,12},{15,13},{18,16},{19,... | collective-permute-start | bytes 147464 | tf_op jit(solution)/shard_map/ppermute | solution.py:15
  9.4 83.1 %collective-permute-start = (bf16[1,1,256,96]{2,3,1,0:T(8,128)(2,1)S(1)}, bf16[1,1,256,96]{2,3,1,0:T(8,128)(2,1)S(1)}, u32[]{:S(2)}, u32[]{:S(2)}) collective-permute-start(bf16[1,1,256,96]{2,3,1,0:T(8,128)(2,1)S(1)} %get-tuple-element.72), channel_id=1, source_target_pairs={{0,2},{1,3},{4,6},{5,7},{8,10},{9,11},{12,14},{13,15},{16,18},{17,... | collective-permute-start | bytes 147464 | tf_op jit(solution)/shard_map/ppermute | solution.py:14
  15.4 80.2 %collective-permute-start.5 = (bf16[1,1,256,96]{2,3,1,0:T(8,128)(2,1)S(1)}, bf16[1,1,256,96]{2,3,1,0:T(8,128)(2,1)S(1)}, u32[]{:S(2)}, u32[]{:S(2)}) collective-permute-start(bf16[1,1,256,96]{2,3,1,0:T(8,128)(2,1)S(1)} %get-tuple-element.69), channel_id=1, source_target_pairs={{2,0},{3,1},{6,4},{7,5},{10,8},{11,9},{14,12},{15,13},{18,16},{19,... | collective-permute-start | bytes 147464 | tf_op jit(solution)/shard_map/ppermute | solution.py:15
  16.7 78.9 %collective-permute-start.4 = (bf16[1,1,256,96]{2,3,1,0:T(8,128)(2,1)S(1)}, bf16[1,1,256,96]{2,3,1,0:T(8,128)(2,1)S(1)}, u32[]{:S(2)}, u32[]{:S(2)}) collective-permute-start(bf16[1,1,256,96]{2,3,1,0:T(8,128)(2,1)S(1)} %get-tuple-element.68), channel_id=1, source_target_pairs={{0,2},{1,3},{4,6},{5,7},{8,10},{9,11},{12,14},{13,15},{16,18},{17,... | collective-permute-start | bytes 147464 | tf_op jit(solution)/shard_map/ppermute | solution.py:14
  22.3 1.1 copy-start.5
  23.4 0.8 copy-start.18
  92.5 19.2 %collective-permute-start.2 = (bf16[1,6,256,96]{2,3,1,0:T(8,128)(2,1)S(1)}, bf16[1,6,256,96]{2,3,1,0:T(8,128)(2,1)S(1)}, u32[]{:S(2)}, u32[]{:S(2)}) collective-permute-start(bf16[1,6,256,96]{2,3,1,0:T(8,128)(2,1)S(1)} %pad_maximum_fusion.17), channel_id=1, source_target_pairs={{8,0},{12,4},{9,1},{13,5},{10,2},{14,6},{11,3},{15,7},{24,16},{28,... | collective-permute-start | bytes 884744 | tf_op jit(solution)/shard_map/ppermute | solution.py:23
  93.8 18.4 %collective-permute-start.3 = (bf16[1,6,256,96]{2,3,1,0:T(8,128)(2,1)S(1)}, bf16[1,6,256,96]{2,3,1,0:T(8,128)(2,1)S(1)}, u32[]{:S(2)}, u32[]{:S(2)}) collective-permute-start(bf16[1,6,256,96]{2,3,1,0:T(8,128)(2,1)S(1)} %pad_maximum_fusion.17), channel_id=1, source_target_pairs={{4,0},{8,4},{12,8},{5,1},{9,5},{13,9},{6,2},{10,6},{14,10},{7,3},{... | collective-permute-start | bytes 884744 | tf_op jit(solution)/shard_map/ppermute | solution.py:23
  95.6 17.3 %collective-permute-start.6 = (bf16[1,6,256,96]{2,3,1,0:T(8,128)(2,1)S(1)}, bf16[1,6,256,96]{2,3,1,0:T(8,128)(2,1)S(1)}, u32[]{:S(2)}, u32[]{:S(2)}) collective-permute-start(bf16[1,6,256,96]{2,3,1,0:T(8,128)(2,1)S(1)} %pad_maximum_fusion.18), channel_id=1, source_target_pairs={{0,8},{4,12},{1,9},{5,13},{2,10},{6,14},{3,11},{7,15},{16,24},{20,... | collective-permute-start | bytes 884744 | tf_op jit(solution)/shard_map/ppermute | solution.py:23
  101.7 18.6 %collective-permute-start.7 = (bf16[1,6,256,96]{2,3,1,0:T(8,128)(2,1)S(1)}, bf16[1,6,256,96]{2,3,1,0:T(8,128)(2,1)S(1)}, u32[]{:S(2)}, u32[]{:S(2)}) collective-permute-start(bf16[1,6,256,96]{2,3,1,0:T(8,128)(2,1)S(1)} %pad_maximum_fusion.18), channel_id=1, source_target_pairs={{0,4},{4,8},{8,12},{1,5},{5,9},{9,13},{2,6},{6,10},{10,14},{3,7},{... | collective-permute-start | bytes 884744 | tf_op jit(solution)/shard_map/ppermute | solution.py:23
  125.8 1.1 copy-start.3
  126.8 1.3 copy-start.12
  126.8 1.6 copy-start.11
  128.1 0.9 copy-start.10
  128.4 1.1 copy-start.1
  128.4 1.1 copy-start.9
  129.0 1.1 copy-start.2
  129.0 1.1 copy-start.8
  129.5 0.9 copy-start.7
  130.1 0.9 copy-start.13
  130.1 1.0 copy-start.14
  130.1 1.1 copy-start.15
  130.1 1.2 copy-start.17
  130.8 1.1 copy-start.6
  130.8 1.1 copy-start.16
Sparse Core Ops, SparseCore 0:
  127.0 94.7 all-reduce.7
where the time goes:
time: 232 us; the launch traced here: 231 us
  waiting for transfers between devices  88.7 us (38%)
  blocking collectives  59.7 us (26%)
  local copies, waits for them, and re-layouts  30.5 us (13%)
  starting transfers between devices  24.8 us (11%)
  between operations  14.9 us (6%)
  matrix products  7.44 us (3%)
  other arithmetic  5.05 us (2%)
    psum x1, waiting for transfers between devices, on_device(): kernel_total = lax.psum(kernel_local, ('tm', 'space', 'dp'))  88.6 us
    psum x1, blocking collectives, on_device(): sketch_total = lax.psum(sketch_terms, ('tm', 'space', 'dp'))  59.7 us
    unnamed x71, local copies, waits for them, and re-layouts  17.4 us
    ppermute x4, starting transfers between devices, passed_along(): return lax.ppermute(block, axis, route)  12.8 us
    ppermute x2, starting transfers between devices, padded(): before = lax.ppermute(last, axis, up)  9.42 us
  transfers between devices with their start and end apart: 9, of which 1 were waited for; matrix products, arithmetic and copies ran while one was open for 13% of the time, Pallas kernels for 0%

commit v1 on v0

--- a/solution.py
+++ b/solution.py
@@ -92,7 +92,7 @@
         * lax.axis_size("space")
         * lax.axis_size("dp")
     )
-    sketch_total = lax.psum(sketch_terms, ("tm", "space", "dp"))
+    sketch_total = jnp.sum(lax.all_gather(sketch_terms, ("tm", "space", "dp")), axis=0)
     kernel_total = lax.psum(kernel_local, ("tm", "space", "dp"))
     sketches = sketch_total / jnp.float32(total_pixels)
     weight_grad = kernel_total * (1.0 / jnp.sqrt(jnp.float32(total_pixels)))

time: 232 us -> 196 us (0.84)
  blocking collectives: 59.7 us -> 22.1 us
    psum x1 -> x0, blocking collectives: 59.7 us -> none  [on_device(): sketch_total = lax.psum(sketch_terms, ('tm', 'space', 'dp'))]
    all_gather x0 -> x1, blocking collectives: none -> 22.1 us  [on_device(): lax.all_gather(sketch_terms, ('tm', 'space', 'dp'))]
  transfers between devices with their start and end apart: 9 -> 9, of which waited for: 1 -> 1; matrix products, arithmetic and copies ran while one was open for 13% -> 16% of each run, Pallas kernels for 0% -> 0%
where the time goes in v1:
time: 196 us
  waiting for transfers between devices  91 us (46%)
  local copies, waits for them, and re-layouts  30.5 us (16%)
  starting transfers between devices  24.8 us (13%)
  blocking collectives  22.1 us (11%)
  between operations  14.9 us (8%)
  matrix products  7.42 us (4%)
  other arithmetic  5.12 us (3%)
    psum x1, waiting for transfers between devices, on_device(): kernel_total = lax.psum(kernel_local, ('tm', 'space', 'dp'))  90.9 us
    all_gather x1, blocking collectives, on_device(): lax.all_gather(sketch_terms, ('tm', 'space', 'dp'))  22.1 us
    unnamed x71, local copies, waits for them, and re-layouts  17.4 us
    ppermute x4, starting transfers between devices, passed_along(): return lax.ppermute(block, axis, route)  12.8 us
    ppermute x2, starting transfers between devices, padded(): before = lax.ppermute(last, axis, up)  9.42 us
  transfers between devices with their start and end apart: 9, of which 1 were waited for; matrix products, arithmetic and copies ran while one was open for 16% of the time, Pallas kernels for 0%

profile of v1, /device:TPU:0, one launch (start us, length us, event | category | flops | bytes accessed | tf_op | source)
XLA Modules:
  0.0 195.8 jit_solution(17880652456468030082)
XLA Ops:
  7.2 0.9 fusion.34
  8.2 1.3 collective-permute-start.1
  9.4 4.9 %collective-permute-start = (bf16[1,1,256,96]{2,3,1,0:T(8,128)(2,1)S(1)}, bf16[1,1,256,96]{2,3,1,0:T(8,128)(2,1)S(1)}, u32[]{:S(2)}, u32[]{:S(2)}) collective-permute-start(bf16[1,1,256,96]{2,3,1,0:T(8,128)(2,1)S(1)} %get-tuple-element.75), channel_id=1, source_target_pairs={{0,2},{1,3},{4,6},{5,7},{8,10},{9,11},{12,14},{13,15},{16,18},{17,... | collective-permute-start | bytes 147464 | tf_op jit(solution)/shard_map/ppermute | solution.py:14
  14.3 1.0 fusion.27
  15.4 1.3 collective-permute-start.5
  16.7 4.5 %collective-permute-start.4 = (bf16[1,1,256,96]{2,3,1,0:T(8,128)(2,1)S(1)}, bf16[1,1,256,96]{2,3,1,0:T(8,128)(2,1)S(1)}, u32[]{:S(2)}, u32[]{:S(2)}) collective-permute-start(bf16[1,1,256,96]{2,3,1,0:T(8,128)(2,1)S(1)} %get-tuple-element.71), channel_id=1, source_target_pairs={{0,2},{1,3},{4,6},{5,7},{8,10},{9,11},{12,14},{13,15},{16,18},{17,... | collective-permute-start | bytes 147464 | tf_op jit(solution)/shard_map/ppermute | solution.py:14
  21.2 1.1 copy.63
  24.6 22.1 %all-gather = f32[32,96,32]{1,2,0:T(8,128)S(1)} all-gather(f32[2,96,32]{1,2,0:T(8,128)S(1)} %pad_maximum_fusion.19), channel_id=2, replica_groups=mesh['groups'=2,'tm'=4,'space'=2,'dp'=2] {'tm','space','dp'}, dimensions={0}, use_global_device_ids=true | all-gather | bytes 417792 | tf_op jit(solution)/shard_map/all_gather | solution.py:95
  47.5 0.7 copy.75
  48.3 0.7 copy.76
  49.0 0.7 copy.77
  49.8 0.7 copy.78
  50.5 0.7 copy.79
  51.2 0.7 copy.80
  52.0 0.7 copy.81
  52.7 0.7 copy.82
  53.5 0.7 copy.92
  54.2 0.7 copy.83
  55.0 1.3 collective-permute-start.2
  56.3 1.3 collective-permute-start.3
  58.1 6.1 %collective-permute-start.6 = (bf16[1,6,256,96]{2,3,1,0:T(8,128)(2,1)S(1)}, bf16[1,6,256,96]{2,3,1,0:T(8,128)(2,1)S(1)}, u32[]{:S(2)}, u32[]{:S(2)}) collective-permute-start(bf16[1,6,256,96]{2,3,1,0:T(8,128)(2,1)S(1)} %pad_maximum_fusion.18), channel_id=1, source_target_pairs={{0,8},{4,12},{1,9},{5,13},{2,10},{6,14},{3,11},{7,15},{16,24},{20,... | collective-permute-start | bytes 884744 | tf_op jit(solution)/shard_map/ppermute | solution.py:23
  64.2 4.1 %collective-permute-start.7 = (bf16[1,6,256,96]{2,3,1,0:T(8,128)(2,1)S(1)}, bf16[1,6,256,96]{2,3,1,0:T(8,128)(2,1)S(1)}, u32[]{:S(2)}, u32[]{:S(2)}) collective-permute-start(bf16[1,6,256,96]{2,3,1,0:T(8,128)(2,1)S(1)} %pad_maximum_fusion.18), channel_id=1, source_target_pairs={{0,4},{4,8},{8,12},{1,5},{5,9},{9,13},{2,6},{6,10},{10,14},{3,7},{... | collective-permute-start | bytes 884744 | tf_op jit(solution)/shard_map/ppermute | solution.py:23
  70.1 0.7 copy.93
  71.0 0.7 copy.91
  72.2 0.9 copy.94
  78.6 0.9 copy.88
  80.0 0.9 copy.89
  88.2 1.1 copy-done.3
  89.3 1.2 fusion.35
  94.8 0.7 copy.74
  95.5 90.9 %all-reduce.8.cloned.1.call-done = f32[3,3,3,96,96]{4,3,2,1,0:T(8,128)} async-done(((f32[3,3,3,96,96]{4,3,2,1,0:T(8,128)}), f32[3,3,3,96,96]{4,3,2,1,0:T(8,128)}) %all-reduce.8.cloned.1.call-update) | async-done | bytes 995344 | tf_op jit(solution)/shard_map/psum | solution.py:96
  186.5 2.5 %broadcast_multiply_fusion = f32[3,3,3,96,96]{4,3,2,1,0:T(8,128)} fusion(f32[3,3,3,96,96]{4,3,2,1,0:T(8,128)} %all-reduce.8.cloned.1.call-done), kind=kLoop, calls=%fused_computation.32 | loop fusion | flops 248832 | bytes 1990656 | tf_op jit(solution)/shard_map/mul | solution.py:98
  (133 shorter events, 23.1 us)
Async XLA Ops:
  7.2 15.2 %copy-start = (bf16[1,1,4,256,96]{3,4,2,1,0:T(8,128)(2,1)S(1)}, bf16[1,1,4,256,96]{3,4,2,1,0:T(8,128)(2,1)}, u32[]{:S(2)}) copy-start(bf16[1,1,4,256,96]{3,4,2,1,0:T(8,128)(2,1)} %param.5) | copy-start | bytes 589828
  7.2 15.4 %copy-start.4 = (bf16[1,1,4,256,96]{3,4,2,1,0:T(8,128)(2,1)S(1)}, bf16[1,1,4,256,96]{3,4,2,1,0:T(8,128)(2,1)}, u32[]{:S(2)}) copy-start(bf16[1,1,4,256,96]{3,4,2,1,0:T(8,128)(2,1)} %param.4) | copy-start | bytes 589828
  7.2 179.3 %all-reduce.8.cloned.1.call-start = ((), (), s32[]{:S(2)}) async-start(), calls=%async_computation | async-start | bytes 2654208 | tf_op jit(solution)/shard_map/psum | solution.py:96
  8.2 46.8 %collective-permute-start.1 = (bf16[1,1,256,96]{2,3,1,0:T(8,128)(2,1)S(1)}, bf16[1,1,256,96]{2,3,1,0:T(8,128)(2,1)S(1)}, u32[]{:S(2)}, u32[]{:S(2)}) collective-permute-start(bf16[1,1,256,96]{2,3,1,0:T(8,128)(2,1)S(1)} %get-tuple-element.76), channel_id=1, source_target_pairs={{2,0},{3,1},{6,4},{7,5},{10,8},{11,9},{14,12},{15,13},{18,16},{19,... | collective-permute-start | bytes 147464 | tf_op jit(solution)/shard_map/ppermute | solution.py:15
  9.4 45.5 %collective-permute-start = (bf16[1,1,256,96]{2,3,1,0:T(8,128)(2,1)S(1)}, bf16[1,1,256,96]{2,3,1,0:T(8,128)(2,1)S(1)}, u32[]{:S(2)}, u32[]{:S(2)}) collective-permute-start(bf16[1,1,256,96]{2,3,1,0:T(8,128)(2,1)S(1)} %get-tuple-element.75), channel_id=1, source_target_pairs={{0,2},{1,3},{4,6},{5,7},{8,10},{9,11},{12,14},{13,15},{16,18},{17,... | collective-permute-start | bytes 147464 | tf_op jit(solution)/shard_map/ppermute | solution.py:14
  15.4 42.6 %collective-permute-start.5 = (bf16[1,1,256,96]{2,3,1,0:T(8,128)(2,1)S(1)}, bf16[1,1,256,96]{2,3,1,0:T(8,128)(2,1)S(1)}, u32[]{:S(2)}, u32[]{:S(2)}) collective-permute-start(bf16[1,1,256,96]{2,3,1,0:T(8,128)(2,1)S(1)} %get-tuple-element.72), channel_id=1, source_target_pairs={{2,0},{3,1},{6,4},{7,5},{10,8},{11,9},{14,12},{15,13},{18,16},{19,... | collective-permute-start | bytes 147464 | tf_op jit(solution)/shard_map/ppermute | solution.py:15
  16.7 41.3 %collective-permute-start.4 = (bf16[1,1,256,96]{2,3,1,0:T(8,128)(2,1)S(1)}, bf16[1,1,256,96]{2,3,1,0:T(8,128)(2,1)S(1)}, u32[]{:S(2)}, u32[]{:S(2)}) collective-permute-start(bf16[1,1,256,96]{2,3,1,0:T(8,128)(2,1)S(1)} %get-tuple-element.71), channel_id=1, source_target_pairs={{0,2},{1,3},{4,6},{5,7},{8,10},{9,11},{12,14},{13,15},{16,18},{17,... | collective-permute-start | bytes 147464 | tf_op jit(solution)/shard_map/ppermute | solution.py:14
  22.3 1.1 copy-start.5
  23.4 0.8 copy-start.18
  55.0 19.2 %collective-permute-start.2 = (bf16[1,6,256,96]{2,3,1,0:T(8,128)(2,1)S(1)}, bf16[1,6,256,96]{2,3,1,0:T(8,128)(2,1)S(1)}, u32[]{:S(2)}, u32[]{:S(2)}) collective-permute-start(bf16[1,6,256,96]{2,3,1,0:T(8,128)(2,1)S(1)} %pad_maximum_fusion.17), channel_id=1, source_target_pairs={{8,0},{12,4},{9,1},{13,5},{10,2},{14,6},{11,3},{15,7},{24,16},{28,... | collective-permute-start | bytes 884744 | tf_op jit(solution)/shard_map/ppermute | solution.py:23
  56.3 18.4 %collective-permute-start.3 = (bf16[1,6,256,96]{2,3,1,0:T(8,128)(2,1)S(1)}, bf16[1,6,256,96]{2,3,1,0:T(8,128)(2,1)S(1)}, u32[]{:S(2)}, u32[]{:S(2)}) collective-permute-start(bf16[1,6,256,96]{2,3,1,0:T(8,128)(2,1)S(1)} %pad_maximum_fusion.17), channel_id=1, source_target_pairs={{4,0},{8,4},{12,8},{5,1},{9,5},{13,9},{6,2},{10,6},{14,10},{7,3},{... | collective-permute-start | bytes 884744 | tf_op jit(solution)/shard_map/ppermute | solution.py:23
  58.1 17.3 %collective-permute-start.6 = (bf16[1,6,256,96]{2,3,1,0:T(8,128)(2,1)S(1)}, bf16[1,6,256,96]{2,3,1,0:T(8,128)(2,1)S(1)}, u32[]{:S(2)}, u32[]{:S(2)}) collective-permute-start(bf16[1,6,256,96]{2,3,1,0:T(8,128)(2,1)S(1)} %pad_maximum_fusion.18), channel_id=1, source_target_pairs={{0,8},{4,12},{1,9},{5,13},{2,10},{6,14},{3,11},{7,15},{16,24},{20,... | collective-permute-start | bytes 884744 | tf_op jit(solution)/shard_map/ppermute | solution.py:23
  64.2 18.6 %collective-permute-start.7 = (bf16[1,6,256,96]{2,3,1,0:T(8,128)(2,1)S(1)}, bf16[1,6,256,96]{2,3,1,0:T(8,128)(2,1)S(1)}, u32[]{:S(2)}, u32[]{:S(2)}) collective-permute-start(bf16[1,6,256,96]{2,3,1,0:T(8,128)(2,1)S(1)} %pad_maximum_fusion.18), channel_id=1, source_target_pairs={{0,4},{4,8},{8,12},{1,5},{5,9},{9,13},{2,6},{6,10},{10,14},{3,7},{... | collective-permute-start | bytes 884744 | tf_op jit(solution)/shard_map/ppermute | solution.py:23
  88.2 1.1 copy-start.3
  89.3 1.3 copy-start.12
  89.3 1.6 copy-start.11
  90.5 0.9 copy-start.10
  90.9 1.1 copy-start.1
  90.9 1.1 copy-start.9
  91.4 1.1 copy-start.2
  91.4 1.1 copy-start.8
  91.9 0.9 copy-start.7
  92.5 0.9 copy-start.13
  92.5 1.0 copy-start.14
  92.5 1.1 copy-start.15
  92.5 1.2 copy-start.17
  93.2 1.1 copy-start.6
  93.2 1.1 copy-start.16
Sparse Core Ops, SparseCore 0:
  89.4 97.0 all-reduce.7
